TPU v7x, 256 devices: a whole 4x4x8 slice. The times are simulated.
256 devices in a mesh: outer: 8 (over z_lo, x), inner: 32 (over z_hi, y, core).
Axes of the slice: x: 4, y: 4, z: 8 (z_hi: 4, z_lo: 2; z = z_hi * 2 + z_lo), core: 2. Of those that a mesh axis runs over, the one named last changes fastest.
Arguments:
- query_stream: float32 [131072, 128], P(('outer', 'inner')), may hold values from -6 to 6
- key_stream: float32 [131072, 128], P(('outer', 'inner')), may hold values from -6 to 6
- value_stream: float32 [131072, 128], P(('outer', 'inner')), may hold values from -6 to 6
- filter_taps: float32 [131072, 128], P(('outer', 'inner')), may hold values from -1.6 to 1.6
- skip_gain: float32 [128], replicated, may hold values from -1 to 1
- short_weights: float32 [3, 3, 128], replicated, may hold values from -3 to 3
- cotangent: float32 [131072, 128], P(('outer', 'inner')), may hold values from -10 to 10
Outputs:
- gated_output: float32 [131072, 128], P(('outer', 'inner'))
- stream_grads: float32 [3, 131072, 128], P(None, ('outer', 'inner'))
- filter_grad: float32 [131072, 128], P(('outer', 'inner'))
- tap_grads: float32 [3, 3, 128], replicated
- skip_grad: float32 [128], replicated
All inputs are finite; a program needn't handle non-finite values.
Results may differ from a plain program's by a relative error of at most 0.0003.
Values sent between devices are 32-bit elements; how exact they have to be, the bound alone decides.
No kernel may reach another device: no remote copies, remote signals or barrier semaphores. Data moves between devices by JAX's collectives and lax.ppermute only.
A program may use at most 64 MiB of HBM per device.

v0:
```python
import math

import jax
import jax.numpy as jnp
from jax import lax
from jax.sharding import PartitionSpec as P

exact_mode = lax.Precision.HIGH
everyone = ("outer", "inner")


def passed_along(block, axis, distance):
    devices = range(lax.axis_size(axis))
    route = [(i - distance, i) for i in devices if i - distance in devices]
    return lax.ppermute(block, axis, route)


def with_partner(block):
    devices = lax.axis_size(everyone)
    return lax.ppermute(block, everyone, [(i, i ^ 1) for i in range(devices)])


def unit_angles(counts_table, period):
    return 2.0 * math.pi / period * (counts_table % period).astype(jnp.float32)


def self_position():
    return lax.axis_index("outer") * lax.axis_size("inner") + lax.axis_index("inner")


def in_halves(first, mine, theirs, axis):
    return jnp.where(
        first,
        jnp.concatenate([mine, theirs], axis=axis),
        jnp.concatenate([theirs, mine], axis=axis),
    )


def dot(left, right):
    return jnp.dot(left, right, precision=exact_mode)


def long_convolutions(pieces, row_count):
    members = len(pieces)
    devices = lax.axis_size(everyone)
    half = row_count // 2
    blocks = 2 * devices
    kept = blocks // 2
    length = blocks * row_count
    position = self_position()
    side = position % 2
    first = side == 0
    hidden_zero = position // (4 * devices)

    block_index = jnp.arange(devices, dtype=jnp.int32) + hidden_zero
    coarse = jnp.arange(blocks, dtype=jnp.int32) + hidden_zero
    fine = jnp.arange(row_count, dtype=jnp.int32) + hidden_zero
    coarse_angles = unit_angles(coarse[:, None] * block_index[None, :], blocks)
    coarse_cos = jnp.cos(coarse_angles)
    coarse_sin = jnp.sin(coarse_angles)
    back_angles = unit_angles(block_index[:, None] * coarse[None, :], blocks)
    back_cos = jnp.cos(back_angles)
    back_sin = jnp.sin(back_angles)
    coarse_mine = side * kept + jnp.arange(kept, dtype=jnp.int32)
    twiddle = unit_angles(coarse_mine[:, None] * fine[None, :], length)[None]
    twiddle_cos = jnp.cos(twiddle)
    twiddle_sin = jnp.sin(twiddle)
    fine_angles = unit_angles(fine[:, None] * fine[None, :], row_count)
    fine_cos = jnp.cos(fine_angles)
    fine_sin = jnp.sin(fine_angles)
    fine_diff = fine_cos - fine_sin
    fine_sum = fine_cos + fine_sin
    tables = (coarse_cos, coarse_sin, back_cos, back_sin, twiddle_cos, twiddle_sin)
    tables += (fine_cos, fine_sin, fine_diff, fine_sum)
    (coarse_cos, coarse_sin, back_cos, back_sin, twiddle_cos, twiddle_sin) = (
        tables := lax.optimization_barrier(tables)
    )[:6]
    fine_cos, fine_sin, fine_diff, fine_sum = tables[6:]

    first_real = jnp.stack([dot(coarse_cos, piece) for piece in pieces])
    first_imag = -jnp.stack([dot(coarse_sin, piece) for piece in pieces])

    def split_coarse(part):
        low, high = part[:, :kept], part[:, kept:]
        return jnp.where(first, low, high), jnp.where(first, high, low)

    keep_real, send_real = split_coarse(first_real)
    keep_imag, send_imag = split_coarse(first_imag)
    got_real, got_imag = with_partner(jnp.stack([send_real, send_imag]))
    full_real = in_halves(first, keep_real, got_real, 2)
    full_imag = in_halves(first, keep_imag, got_imag, 2)

    turned_real = full_real * twiddle_cos + full_imag * twiddle_sin
    turned_imag = full_imag * twiddle_cos - full_real * twiddle_sin

    flat = (members * kept, row_count)
    shape = (members, kept, row_count)
    turned_real = turned_real.reshape(flat)
    turned_imag = turned_imag.reshape(flat)
    real_cos = dot(turned_real, fine_cos)
    imag_sin = dot(turned_imag, fine_sin)
    both = dot(turned_real + turned_imag, fine_diff)
    spec_real = (real_cos + imag_sin).reshape(shape)
    spec_imag = (both - real_cos + imag_sin).reshape(shape)

    filter_real, product_real, upstream_real = (spec_real[0], spec_real[1], spec_real[2])
    filter_imag, product_imag, upstream_imag = (spec_imag[0], spec_imag[1], spec_imag[2])
    causal_real = filter_real * product_real - filter_imag * product_imag
    causal_imag = filter_real * product_imag + filter_imag * product_real
    back_real = filter_real * upstream_real + filter_imag * upstream_imag
    back_imag = filter_real * upstream_imag - filter_imag * upstream_real
    grad_real = product_real * upstream_real + product_imag * upstream_imag
    grad_imag = product_real * upstream_imag - product_imag * upstream_real
    out_real = jnp.stack([causal_real, back_real, grad_real]).reshape(flat)
    out_imag = jnp.stack([causal_imag, back_imag, grad_imag]).reshape(flat)

    real_cos = dot(out_real, fine_cos)
    imag_sin = dot(out_imag, fine_sin)
    both = dot(out_real + out_imag, fine_sum)
    inner_real = (real_cos - imag_sin).reshape(shape)
    inner_imag = (both - real_cos - imag_sin).reshape(shape)
    unturned_real = inner_real * twiddle_cos - inner_imag * twiddle_sin
    unturned_imag = inner_imag * twiddle_cos + inner_real * twiddle_sin

    def split_fine(part):
        low, high = part[:, :, :half], part[:, :, half:]
        return jnp.where(first, low, high), jnp.where(first, high, low)

    mine_real, away_real = split_fine(unturned_real)
    mine_imag, away_imag = split_fine(unturned_imag)
    came_real, came_imag = with_partner(jnp.stack([away_real, away_imag]))
    whole_real = in_halves(first, mine_real, came_real, 1)
    whole_imag = in_halves(first, mine_imag, came_imag, 1)

    scale = 1.0 / length
    return [
        (dot(back_cos, whole_real[m]) - dot(back_sin, whole_imag[m])) * scale
        for m in range(members)
    ]


def on_device(
    query_stream, key_stream, value_stream, filter_taps, skip_gain, short_weights, cotangent
):
    row_count, channels = query_stream.shape
    devices = lax.axis_size(everyone)
    half = row_count // 2
    lane = 128
    position = self_position()
    channel = position // 2

    streams = jnp.stack([query_stream, key_stream, value_stream])
    earlier = passed_along(streams[:, row_count - 2 :, :], everyone, 1)
    ahead = jnp.concatenate([earlier, streams], axis=1)
    mixed = (
        short_weights[:, 0:1] * streams
        + short_weights[:, 1:2] * ahead[:, 1 : row_count + 1]
        + short_weights[:, 2:3] * ahead[:, 0:row_count]
    )

    def by_channel(block):
        return block.reshape(2, half, channels).transpose(2, 0, 1)

    halo = jnp.stack([ahead[:, 0:2], ahead[:, half : half + 2]], axis=1)
    halo = halo.transpose(3, 1, 0, 2).reshape(channels, 2, 6)
    halo = jnp.pad(halo, ((0, 0), (0, 0), (0, lane - 6)))
    sent = jnp.concatenate(
        [by_channel(b) for b in (query_stream, key_stream, value_stream, filter_taps, cotangent)]
        + [halo],
        axis=2,
    ).reshape(devices, -1)
    columns = lax.all_to_all(sent, everyone, 0, 0, tiled=True)

    parts = [columns[:, k * half : (k + 1) * half] for k in range(5)]
    own = jnp.stack(parts[:3])
    filter_part, cotangent_part = parts[3], parts[4]
    before = columns[:, 5 * half : 5 * half + 6].reshape(devices, 3, 2).transpose(1, 0, 2)
    padded = jnp.concatenate([before, own], axis=2)
    lag_one = padded[:, :, 1 : half + 1]
    lag_two = padded[:, :, 0:half]
    weights = lax.dynamic_index_in_dim(short_weights, channel, axis=2, keepdims=False)
    gain = lax.dynamic_index_in_dim(skip_gain, channel, axis=0, keepdims=False)
    mixed_part = (
        weights[:, 0:1, None] * own
        + weights[:, 1:2, None] * lag_one
        + weights[:, 2:3, None] * lag_two
    )
    product = mixed_part[1] * mixed_part[2]
    upstream = cotangent_part * mixed_part[0]
    causal, backward_long, gradient = long_convolutions(
        [filter_part, product, upstream], row_count
    )
    summed_part = causal + gain * product
    backward_part = backward_long + gain * upstream
    grads_part = jnp.stack(
        [cotangent_part * summed_part, backward_part * mixed_part[2], backward_part * mixed_part[1]]
    )
    tap_terms = jnp.stack(
        [
            jnp.sum(grads_part * own, axis=(1, 2)),
            jnp.sum(grads_part * lag_one, axis=(1, 2)),
            jnp.sum(grads_part * lag_two, axis=(1, 2)),
        ],
        axis=1,
    )
    skip_terms = jnp.sum(upstream * product)
    partials = jnp.concatenate([tap_terms.reshape(-1), skip_terms[None]])
    factor = 1.0 / math.sqrt(row_count * devices)
    totals = (partials + with_partner(partials)) * factor
    following = grads_part[:, :, 0:2]
    following = jnp.concatenate([following[:, 1:], jnp.zeros_like(following[:, :1])], axis=1)
    extra = jnp.concatenate(
        [
            jnp.broadcast_to(totals[None], (devices, totals.shape[0])),
            following.transpose(1, 0, 2).reshape(devices, 6),
        ],
        axis=1,
    )
    extra = jnp.pad(extra, ((0, 0), (0, lane - extra.shape[1])))

    payload = jnp.concatenate([summed_part, backward_part, gradient * factor, extra], axis=1)
    returned = lax.all_to_all(payload, everyone, 0, 0, tiled=True)
    summed, backward, filter_grad = (
        returned[:, : 3 * half]
        .reshape(channels, 2, 3, half)
        .transpose(2, 1, 3, 0)
        .reshape(3, row_count, channels)
    )
    extra = returned[:, 3 * half : 3 * half + 16].reshape(channels, 2, 16)[:, 0]
    per_channel = extra[:, :10].T
    later = extra[:, 10:16].reshape(channels, 3, 2).transpose(1, 2, 0)
    tap_total = per_channel[:-1].reshape(3, 3, channels)
    skip_total = per_channel[-1]

    gated_output = mixed[0] * summed
    grads = jnp.stack([cotangent * summed, backward * mixed[2], backward * mixed[1]])
    behind = jnp.concatenate([grads, later], axis=1)
    stream_grads = (
        short_weights[:, 0:1] * grads
        + short_weights[:, 1:2] * behind[:, 1 : row_count + 1]
        + short_weights[:, 2:3] * behind[:, 2 : row_count + 2]
    )
    return (gated_output, stream_grads, filter_grad, tap_total, skip_total)


def solution(mesh):
    placed = (
        P(everyone, None),
        P(everyone, None),
        P(everyone, None),
        P(everyone, None),
        P(),
        P(),
        P(everyone, None),
    )
    return jax.shard_map(
        on_device,
        mesh=mesh,
        in_specs=placed,
        out_specs=(
            P(everyone, None),
            P(None, everyone, None),
            P(everyone, None),
            P(),
            P(),
        ),
        check_vma=False,
    )
```

profile of v0, /device:TPU:1, one launch (start us, length us, event | category | flops | bytes accessed | tf_op | source)
XLA Modules:
  0.0 155.5 jit_solution(10927436653940196093)
XLA Ops:
  0.7 1.2 pad_maximum_fusion.6
  1.9 4.7 %collective-permute-start = (f32[3,2,128]{2,1,0:T(2,128)S(1)}, f32[3,2,128]{2,1,0:T(2,128)S(1)}, u32[]{:S(2)}, u32[]{:S(2)}) collective-permute-start(f32[3,2,128]{2,1,0:T(2,128)S(1)} %get-tuple-element.83), channel_id=1, source_target_pairs={{0,1},{1,2},{2,3},{3,4},{4,5},{5,6},{6,7},{7,8},{8,9},{9,10},{10,1... | collective-permute-start | bytes 9224 | tf_op jit(solution)/shard_map/ppermute | solution.py:15
  8.1 3.2 %all_to_all.22 = f32[256,1,1408]{2,1,0:T(1,128)} reshape(f32[128,2,1408]{2,1,0:T(2,128)S(1)} %pad_dynamic-update-slice_fusion) | data formatting | bytes 2883584 | tf_op jit(solution)/shard_map/all_to_all | solution.py:172
  11.4 17.2 %all-to-all-start = ((f32[256,1,1408]{2,1,0:T(1,128)}), f32[256,1,1408]{2,1,0:T(1,128)}, u32[]{:S(2)}, u32[]{:S(2)}) async-start(f32[256,1,1408]{2,1,0:T(1,128)} %all_to_all.22), calls=%async_computation | async-start | bytes 2883584 | tf_op jit(solution)/shard_map/all_to_all | solution.py:172
  28.7 3.1 %fusion.43 = (f32[256,512]{1,0:T(8,128)}, f32[256,512]{1,0:T(8,128)S(1)}) fusion(s32[512]{0:T(512)S(1)} %iota_add_fusion, s32[256]{0:T(256)S(1)} %iota_add_fusion.2), kind=kLoop, calls=%fused_computation.145 | loop fusion | flops 1835008 | bytes 1051648 | tf_op jit(solution)/shard_map/sin | solution.py:63
  31.8 3.1 %fusion.45 = (f32[512,256]{1,0:T(8,128)S(1)}, f32[512,256]{1,0:T(8,128)}) fusion(s32[256]{0:T(256)S(1)} %iota_add_fusion.2, s32[512]{0:T(512)S(1)} %iota_add_fusion), kind=kLoop, calls=%fused_computation.147 | loop fusion | flops 1835008 | bytes 1051648 | tf_op jit(solution)/shard_map/sin | solution.py:60
  34.9 3.2 %fusion.41 = (f32[1,256,512]{2,1,0:T(8,128)}, f32[1,256,512]{2,1,0:T(8,128)}) fusion(s32[512]{0:T(512)S(1)} %iota_add_fusion, s32[256]{0:T(256)S(1)} %iota_add_fusion.1), kind=kLoop, calls=%fused_computation.143 | loop fusion | flops 1835008 | bytes 1051648 | tf_op jit(solution)/shard_map/sin | solution.py:67
  38.2 5.9 %fusion.37 = (f32[512,512]{1,0:T(8,128)}, f32[512,512]{1,0:T(8,128)}, f32[512,512]{1,0:T(8,128)S(1)}, f32[512,512]{1,0:T(8,128)S(1)}) fusion(s32[512]{0:T(512)S(1)} %iota_add_fusion), kind=kLoop, calls=%fused_computation.120 | loop fusion | flops 4194304 | bytes 4196352 | tf_op jit(solution)/shard_map/add | solution.py:72
  44.2 0.2 slice_reduce_fusion.3
  44.4 22.9 %all-to-all-done = f32[256,1,1408]{2,1,0:T(1,128)} async-done(((f32[256,1,1408]{2,1,0:T(1,128)}), f32[256,1,1408]{2,1,0:T(1,128)}, u32[]{:S(2)}, u32[]{:S(2)}) %all-to-all-start) | async-done | bytes 1441824 | tf_op jit(solution)/shard_map/all_to_all | solution.py:172
  67.2 4.7 %copy.67 = f32[256,1,1408]{0,2,1:T(8,128)} copy(f32[256,1,1408]{2,1,0:T(1,128)} %all-to-all-done) | data formatting | bytes 2883584 | tf_op jit(solution)/shard_map/all_to_all | solution.py:172
  72.0 2.0 %slice_bitcast_fusion.19 = (f32[1,256,256]{1,2,0:T(8,128)S(1)}, f32[1,256,256]{1,2,0:T(8,128)}, f32[1,256,256]{1,2,0:T(8,128)}) fusion(f32[256,1408]{0,1:T(8,128)} %bitcast.209), kind=kLoop, calls=%fused_computation.130 | loop fusion | bytes 1572864 | tf_op jit(solution)/shard_map/stack | solution.py:175
  74.0 0.7 slice.241
  74.7 2.2 %convolution_bitcast_fusion.5 = f32[1,512,256]{2,1,0:T(8,128)} fusion(f32[512,256]{1,0:T(8,128)S(1)} %copy-done, f32[256,1408]{0,1:T(8,128)} %bitcast.211), kind=kOutput, calls=%fused_computation.34 | convolution fusion | flops 201326592 | bytes 1310720 | tf_op jit(solution)/shard_map/dot_general | solution.py:40
  76.9 1.1 maximum_maximum_fusion
  78.1 0.3 multiply_add_fusion.1
  78.3 1.1 copy-done.3
  79.4 0.7 multiply_reduce_fusion.3
  80.1 0.4 copy-done.1
  80.5 0.4 convolution_bitcast_fusion.4
  80.9 0.4 convolution_bitcast_fusion.2
  81.3 0.4 convolution_bitcast_fusion.1
  81.7 0.4 convolution_bitcast_fusion.3
  82.2 0.4 convolution_bitcast_fusion
  82.6 0.2 copy-done.16
  83.6 0.9 collective-permute-start.1
  84.5 3.0 %collective-permute-done.1 = f32[2,3,256,256]{3,2,1,0:T(8,128)S(1)} collective-permute-done((f32[2,3,256,256]{3,2,1,0:T(8,128)S(1)}, f32[2,3,256,256]{3,2,1,0:T(8,128)S(1)}, u32[]{:S(2)}, u32[]{:S(2)}) %collective-permute-start.1) | collective-permute-done | bytes 1572896 | tf_op jit(solution)/shard_map/ppermute | solution.py:20
  87.8 0.7 fusion
  88.5 1.4 fusion.57
  90.0 1.4 fusion.55
  91.4 1.5 subtract_add_fusion
  93.0 0.4 subtract_bitcast_fusion.2
  93.3 0.5 add_bitcast_fusion
  94.0 1.4 fusion.58
  95.6 1.5 fusion.56
  97.1 1.6 %subtract_subtract_fusion = f32[768,512]{1,0:T(8,128)S(1)} fusion(f32[768,512]{1,0:T(8,128)S(1)} %fusion.58, f32[768,512]{1,0:T(8,128)S(1)} %get-tuple-element.102, f32[512,512]{1,0:T(8,128)S(1)} %copy-done.6, f32[768,512]{1,0:T(8,128)S(1)} %bitcast.206, f32[768,512]{1,0:T(8,128)S(1)} %bitcast.208), kind=kOutput, calls=%fused_computation.21 | convolution fusion | flops 1209139200 | bytes 8912896 | tf_op jit(solution)/shard_map/dot_general | solution.py:40
  98.7 0.7 multiply_subtract_fusion
  99.9 0.7 collective-permute-start.2
  100.6 0.6 dynamic_slice.9
  101.2 2.5 %collective-permute-done.2 = f32[2,3,256,256]{3,2,1,0:T(8,128)S(1)} collective-permute-done((f32[2,3,256,256]{3,2,1,0:T(8,128)S(1)}, f32[2,3,256,256]{3,2,1,0:T(8,128)S(1)}, u32[]{:S(2)}, u32[]{:S(2)}) %collective-permute-start.2) | collective-permute-done | bytes 1572896 | tf_op jit(solution)/shard_map/ppermute | solution.py:20
  103.7 0.4 maximum_select_fusion.2
  104.1 0.6 fusion.32
  104.8 0.6 fusion.34
  105.4 0.6 fusion.33
  106.0 0.6 fusion.14
  106.6 1.2 fusion.11
  107.9 1.2 fusion.13
  109.2 0.4 multiply_reduce_fusion.1
  109.8 0.7 pad_maximum_fusion.11
  110.5 0.4 collective-permute-start.3
  111.0 0.7 collective-permute-done.3
  111.8 0.7 add_multiply_fusion
  112.7 2.4 %copy.69 = f32[256,1,896]{2,1,0:T(1,128)} copy(f32[256,1,896]{0,2,1:T(8,128)S(1)} %fusion.18) | data formatting | bytes 1835008 | tf_op jit(solution)/shard_map/all_to_all | solution.py:222
  115.1 5.4 %all-to-all-start.1 = ((f32[256,1,896]{2,1,0:T(1,128)}), f32[256,1,896]{2,1,0:T(1,128)S(1)}, u32[]{:S(2)}, u32[]{:S(2)}) async-start(f32[256,1,896]{2,1,0:T(1,128)} %copy.69), calls=%async_computation.1 | async-start | bytes 1835008 | tf_op jit(solution)/shard_map/all_to_all | solution.py:222
  120.6 0.2 fusion.21
  120.8 28.1 %all-to-all-done.1 = f32[256,1,896]{2,1,0:T(1,128)S(1)} async-done(((f32[256,1,896]{2,1,0:T(1,128)}), f32[256,1,896]{2,1,0:T(1,128)S(1)}, u32[]{:S(2)}, u32[]{:S(2)}) %all-to-all-start.1) | async-done | bytes 917536 | tf_op jit(solution)/shard_map/all_to_all | solution.py:222
  149.2 0.4 reshape.287
  149.7 0.5 fusion.53
  150.7 0.5 copy-done.18
  151.2 0.7 bitcast_multiply_fusion.4
  152.1 1.1 fusion.19
  153.2 0.9 copy.77
  154.1 0.7 slice_reduce_fusion
  154.8 0.6 reshape.290
  (101 shorter events, 4.8 us)
Async XLA Ops:
  0.6 6.0 %copy-start.10 = (f32[512,128]{1,0:T(8,128)S(1)}, f32[512,128]{1,0:T(8,128)}, u32[]{:S(2)}) copy-start(f32[512,128]{1,0:T(8,128)} %param.7) | copy-start | bytes 786436
  0.6 6.2 %copy-start.12 = (f32[512,128]{1,0:T(8,128)S(1)}, f32[512,128]{1,0:T(8,128)}, u32[]{:S(2)}) copy-start(f32[512,128]{1,0:T(8,128)} %param.8) | copy-start | bytes 786436
  0.7 6.4 %copy-start.14 = (f32[512,128]{1,0:T(8,128)S(1)}, f32[512,128]{1,0:T(8,128)}, u32[]{:S(2)}) copy-start(f32[512,128]{1,0:T(8,128)} %param.9) | copy-start | bytes 786436
  0.7 6.6 %copy-start.19 = (f32[512,128]{1,0:T(8,128)S(1)}, f32[512,128]{1,0:T(8,128)}, u32[]{:S(2)}) copy-start(f32[512,128]{1,0:T(8,128)} %param.10) | copy-start | bytes 786436
  1.9 5.5 %copy-start.17 = (f32[512,128]{1,0:T(8,128)S(1)}, f32[512,128]{1,0:T(8,128)}, u32[]{:S(2)}) copy-start(f32[512,128]{1,0:T(8,128)} %param.13) | copy-start | bytes 786436
  1.9 5.9 %collective-permute-start = (f32[3,2,128]{2,1,0:T(2,128)S(1)}, f32[3,2,128]{2,1,0:T(2,128)S(1)}, u32[]{:S(2)}, u32[]{:S(2)}) collective-permute-start(f32[3,2,128]{2,1,0:T(2,128)S(1)} %get-tuple-element.83), channel_id=1, source_target_pairs={{0,1},{1,2},{2,3},{3,4},{4,5},{5,6},{6,7},{7,8},{8,9},{9,10},{10,1... | collective-permute-start | bytes 9224 | tf_op jit(solution)/shard_map/ppermute | solution.py:15
  11.4 55.9 %all-to-all-start = ((f32[256,1,1408]{2,1,0:T(1,128)}), f32[256,1,1408]{2,1,0:T(1,128)}, u32[]{:S(2)}, u32[]{:S(2)}) async-start(f32[256,1,1408]{2,1,0:T(1,128)} %all_to_all.22), calls=%async_computation | async-start | bytes 2883584 | tf_op jit(solution)/shard_map/all_to_all | solution.py:172
  38.2 5.9 %copy-start.20 = (f32[3,3,128]{2,1,0:T(4,128)S(1)}, f32[3,3,128]{2,1,0:T(4,128)}, u32[]{:S(2)}) copy-start(f32[3,3,128]{2,1,0:T(4,128)} %param.12) | copy-start | bytes 13828
  72.0 2.7 %copy-start = (f32[512,256]{1,0:T(8,128)S(1)}, f32[512,256]{1,0:T(8,128)}, u32[]{:S(2)}) copy-start(f32[512,256]{1,0:T(8,128)} %get-tuple-element.16) | copy-start | bytes 1572868
  76.9 1.2 copy-start.8
  76.9 1.2 copy-start.9
  78.1 1.4 copy-start.3
  79.4 1.0 copy-start.1
  81.7 1.0 copy-start.16
  83.6 4.2 %copy-start.4 = (f32[1,256,512]{2,1,0:T(8,128)S(1)}, f32[1,256,512]{2,1,0:T(8,128)}, u32[]{:S(2)}) copy-start(f32[1,256,512]{2,1,0:T(8,128)} %get-tuple-element.19) | copy-start | bytes 1572868
  83.6 4.2 %copy-start.5 = (f32[1,256,512]{2,1,0:T(8,128)S(1)}, f32[1,256,512]{2,1,0:T(8,128)}, u32[]{:S(2)}) copy-start(f32[1,256,512]{2,1,0:T(8,128)} %get-tuple-element.18) | copy-start | bytes 1572868
  83.6 4.0 %collective-permute-start.1 = (f32[2,3,256,256]{3,2,1,0:T(8,128)S(1)}, f32[2,3,256,256]{3,2,1,0:T(8,128)S(1)}, u32[]{:S(2)}, u32[]{:S(2)}) collective-permute-start(f32[2,3,256,256]{3,2,1,0:T(8,128)S(1)} %pad_maximum_fusion.1), channel_id=1, source_target_pairs={{0,1},{1,0},{2,3},{3,2},{4,5},{5,4},{6,7},{7,6},{8,9},{9,8},{10,11... | collective-permute-start | bytes 4718600 | tf_op jit(solution)/shard_map/ppermute | solution.py:20
  89.9 1.5 copy-start.7
  95.5 1.5 copy-start.6
  99.7 0.9 copy-start.21
  99.9 3.7 %collective-permute-start.2 = (f32[2,3,256,256]{3,2,1,0:T(8,128)S(1)}, f32[2,3,256,256]{3,2,1,0:T(8,128)S(1)}, u32[]{:S(2)}, u32[]{:S(2)}) collective-permute-start(f32[2,3,256,256]{3,2,1,0:T(8,128)S(1)} %pad_maximum_fusion.4), channel_id=1, source_target_pairs={{0,1},{1,0},{2,3},{3,2},{4,5},{5,4},{6,7},{7,6},{8,9},{9,8},{10,11... | collective-permute-start | bytes 4718600 | tf_op jit(solution)/shard_map/ppermute | solution.py:20
  104.7 1.2 copy-start.2
  110.5 1.2 collective-permute-start.3
  112.6 7.9 %copy-start.11 = (f32[512,128]{1,0:T(8,128)S(1)}, f32[512,128]{1,0:T(8,128)}, u32[]{:S(2)}) copy-start(f32[512,128]{1,0:T(8,128)} %param.7) | copy-start | bytes 786436
  112.6 7.9 %copy-start.13 = (f32[512,128]{1,0:T(8,128)S(1)}, f32[512,128]{1,0:T(8,128)}, u32[]{:S(2)}) copy-start(f32[512,128]{1,0:T(8,128)} %param.8) | copy-start | bytes 786436
  112.7 7.9 %copy-start.15 = (f32[512,128]{1,0:T(8,128)S(1)}, f32[512,128]{1,0:T(8,128)}, u32[]{:S(2)}) copy-start(f32[512,128]{1,0:T(8,128)} %param.9) | copy-start | bytes 786436
  115.1 33.9 %all-to-all-start.1 = ((f32[256,1,896]{2,1,0:T(1,128)}), f32[256,1,896]{2,1,0:T(1,128)S(1)}, u32[]{:S(2)}, u32[]{:S(2)}) async-start(f32[256,1,896]{2,1,0:T(1,128)} %copy.69), calls=%async_computation.1 | async-start | bytes 1835008 | tf_op jit(solution)/shard_map/all_to_all | solution.py:222
  150.2 1.0 copy-start.18
where the time goes:
time: 156 us; the launch traced here: 155 us
  waiting for transfers between devices  57.2 us (37%)
  starting transfers between devices  29.4 us (19%)
  other arithmetic  27.2 us (17%)
  local copies, waits for them, and re-layouts  22.1 us (14%)
  matrix products  18.1 us (12%)
    all_to_all x1, waiting for transfers between devices, on_device(): returned = lax.all_to_all(payload, everyone, 0, 0, tiled=True)  28.1 us
    all_to_all x1, waiting for transfers between devices, on_device(): columns = lax.all_to_all(sent, everyone, 0, 0, tiled=True)  22.9 us
    dot_general x18, matrix products, dot(): return jnp.dot(left, right, precision=exact_mode)  18.1 us
    all_to_all x1, starting transfers between devices, on_device(): columns = lax.all_to_all(sent, everyone, 0, 0, tiled=True)  17.2 us
    all_to_all x2, local copies, waits for them, and re-layouts, on_device(): columns = lax.all_to_all(sent, everyone, 0, 0, tiled=True)  7.97 us
    ppermute x3, waiting for transfers between devices, with_partner(): return lax.ppermute(block, everyone, [(i, i ^ 1) for i in range(devices)])  6.21 us
    add x1, other arithmetic, long_convolutions(): fine_sum = fine_cos + fine_sin  5.85 us
    all_to_all x1, starting transfers between devices, on_device(): returned = lax.all_to_all(payload, everyone, 0, 0, tiled=True)  5.41 us
  transfers between devices with their start and end apart: 6, of which 5 were waited for; matrix products, arithmetic and copies ran while one was open for 11% of the time, Pallas kernels for 0%

commit v1 on v0

--- a/solution.py
+++ b/solution.py
@@ -86,9 +86,9 @@
 
     keep_real, send_real = split_coarse(first_real)
     keep_imag, send_imag = split_coarse(first_imag)
-    got_real, got_imag = with_partner(jnp.stack([send_real, send_imag]))
-    full_real = in_halves(first, keep_real, got_real, 2)
-    full_imag = in_halves(first, keep_imag, got_imag, 2)
+    got = [with_partner(jnp.stack([send_real[m], send_imag[m]])) for m in range(members)]
+    full_real = in_halves(first, keep_real, jnp.stack([g[0] for g in got]), 2)
+    full_imag = in_halves(first, keep_imag, jnp.stack([g[1] for g in got]), 2)
 
     turned_real = full_real * twiddle_cos + full_imag * twiddle_sin
     turned_imag = full_imag * twiddle_cos - full_real * twiddle_sin
@@ -128,15 +128,14 @@
 
     mine_real, away_real = split_fine(unturned_real)
     mine_imag, away_imag = split_fine(unturned_imag)
-    came_real, came_imag = with_partner(jnp.stack([away_real, away_imag]))
-    whole_real = in_halves(first, mine_real, came_real, 1)
-    whole_imag = in_halves(first, mine_imag, came_imag, 1)
-
     scale = 1.0 / length
-    return [
-        (dot(back_cos, whole_real[m]) - dot(back_sin, whole_imag[m])) * scale
-        for m in range(members)
-    ]
+    outputs = []
+    for m in range(members):
+        came_real, came_imag = with_partner(jnp.stack([away_real[m], away_imag[m]]))
+        whole_real = in_halves(first, mine_real[m], came_real, 0)
+        whole_imag = in_halves(first, mine_imag[m], came_imag, 0)
+        outputs.append((dot(back_cos, whole_real) - dot(back_sin, whole_imag)) * scale)
+    return outputs
 
 
 def on_device(

time: 156 us -> 157 us (level)
  waiting for transfers between devices: 57.2 us -> 54.6 us
  local copies, waits for them, and re-layouts: 22.1 us -> 24.4 us
    ppermute x3 -> x7, waiting for transfers between devices: 6.21 us -> 2.76 us  [with_partner(): return lax.ppermute(block, everyone, [(i, i ^ 1) for i in range(devices)])]
    ppermute x3 -> x7, starting transfers between devices: 2.02 us -> 3.39 us  [with_partner(): return lax.ppermute(block, everyone, [(i, i ^ 1) for i in range(devices)])]
  transfers between devices with their start and end apart: 6 -> 10, of which waited for: 5 -> 5; matrix products, arithmetic and copies ran while one was open for 11% -> 16% of each run, Pallas kernels for 0% -> 0%
where the time goes in v1:
time: 157 us; the launch traced here: 156 us
  waiting for transfers between devices  54.6 us (35%)
  starting transfers between devices  30.6 us (19%)
  other arithmetic  26.7 us (17%)
  local copies, waits for them, and re-layouts  24.4 us (16%)
  matrix products  18 us (11%)
    all_to_all x1, waiting for transfers between devices, on_device(): returned = lax.all_to_all(payload, everyone, 0, 0, tiled=True)  28.1 us
    all_to_all x1, waiting for transfers between devices, on_device(): columns = lax.all_to_all(sent, everyone, 0, 0, tiled=True)  23.7 us
    dot_general x18, matrix products, dot(): return jnp.dot(left, right, precision=exact_mode)  18 us
    all_to_all x1, starting transfers between devices, on_device(): columns = lax.all_to_all(sent, everyone, 0, 0, tiled=True)  17.3 us
    all_to_all x2, local copies, waits for them, and re-layouts, on_device(): columns = lax.all_to_all(sent, everyone, 0, 0, tiled=True)  7.98 us
    add x1, other arithmetic, long_convolutions(): fine_sum = fine_cos + fine_sin  5.88 us
    all_to_all x1, starting transfers between devices, on_device(): returned = lax.all_to_all(payload, everyone, 0, 0, tiled=True)  5.21 us
    unnamed x54, local copies, waits for them, and re-layouts  4.74 us
  transfers between devices with their start and end apart: 10, of which 5 were waited for; matrix products, arithmetic and copies ran while one was open for 16% of the time, Pallas kernels for 0%

profile of v1, /device:TPU:1, one launch (start us, length us, event | category | flops | bytes accessed | tf_op | source)
XLA Modules:
  0.0 155.9 jit_solution(9299203488106742339)
XLA Ops:
  0.7 1.2 pad_maximum_fusion.4
  1.9 4.7 %collective-permute-start = (f32[3,2,128]{2,1,0:T(2,128)S(1)}, f32[3,2,128]{2,1,0:T(2,128)S(1)}, u32[]{:S(2)}, u32[]{:S(2)}) collective-permute-start(f32[3,2,128]{2,1,0:T(2,128)S(1)} %get-tuple-element.97), channel_id=1, source_target_pairs={{0,1},{1,2},{2,3},{3,4},{4,5},{5,6},{6,7},{7,8},{8,9},{9,10},{10,1... | collective-permute-start | bytes 9224 | tf_op jit(solution)/shard_map/ppermute | solution.py:15
  8.1 3.3 %all_to_all.22 = f32[256,1,1408]{2,1,0:T(1,128)} reshape(f32[128,2,1408]{2,1,0:T(2,128)S(1)} %pad_dynamic-update-slice_fusion) | data formatting | bytes 2883584 | tf_op jit(solution)/shard_map/all_to_all | solution.py:171
  11.4 17.3 %all-to-all-start = ((f32[256,1,1408]{2,1,0:T(1,128)}), f32[256,1,1408]{2,1,0:T(1,128)}, u32[]{:S(2)}, u32[]{:S(2)}) async-start(f32[256,1,1408]{2,1,0:T(1,128)} %all_to_all.22), calls=%async_computation | async-start | bytes 2883584 | tf_op jit(solution)/shard_map/all_to_all | solution.py:171
  28.7 2.1 %fusion.73 = (f32[256,512]{1,0:T(8,128)S(1)}, f32[256,512]{1,0:T(8,128)S(1)}) fusion(s32[512]{0:T(512)S(1)} %iota_add_fusion, s32[256]{0:T(256)S(1)} %iota_add_fusion.2), kind=kLoop, calls=%fused_computation.189 | loop fusion | flops 1835008 | bytes 1051648 | tf_op jit(solution)/shard_map/sin | solution.py:63
  30.9 3.2 %fusion.75 = (f32[512,256]{1,0:T(8,128)}, f32[512,256]{1,0:T(8,128)}) fusion(s32[256]{0:T(256)S(1)} %iota_add_fusion.2, s32[512]{0:T(512)S(1)} %iota_add_fusion), kind=kLoop, calls=%fused_computation.191 | loop fusion | flops 1835008 | bytes 1051648 | tf_op jit(solution)/shard_map/sin | solution.py:60
  34.1 3.2 %fusion.71 = (f32[1,256,512]{2,1,0:T(8,128)}, f32[1,256,512]{2,1,0:T(8,128)}) fusion(s32[512]{0:T(512)S(1)} %iota_add_fusion, s32[256]{0:T(256)S(1)} %iota_add_fusion.1), kind=kLoop, calls=%fused_computation.187 | loop fusion | flops 1835008 | bytes 1051648 | tf_op jit(solution)/shard_map/sin | solution.py:67
  37.3 5.9 %fusion.67 = (f32[512,512]{1,0:T(8,128)}, f32[512,512]{1,0:T(8,128)}, f32[512,512]{1,0:T(8,128)S(1)}, f32[512,512]{1,0:T(8,128)S(1)}) fusion(s32[512]{0:T(512)S(1)} %iota_add_fusion), kind=kLoop, calls=%fused_computation.152 | loop fusion | flops 4194304 | bytes 4196352 | tf_op jit(solution)/shard_map/add | solution.py:72
  43.6 23.7 %all-to-all-done = f32[256,1,1408]{2,1,0:T(1,128)} async-done(((f32[256,1,1408]{2,1,0:T(1,128)}), f32[256,1,1408]{2,1,0:T(1,128)}, u32[]{:S(2)}, u32[]{:S(2)}) %all-to-all-start) | async-done | bytes 1441824 | tf_op jit(solution)/shard_map/all_to_all | solution.py:171
  67.3 4.7 %copy.67 = f32[256,1,1408]{0,2,1:T(8,128)} copy(f32[256,1,1408]{2,1,0:T(1,128)} %all-to-all-done) | data formatting | bytes 2883584 | tf_op jit(solution)/shard_map/all_to_all | solution.py:171
  72.0 2.0 %slice_bitcast_fusion.17 = (f32[1,256,256]{1,2,0:T(8,128)S(1)}, f32[1,256,256]{1,2,0:T(8,128)}, f32[1,256,256]{1,2,0:T(8,128)}) fusion(f32[256,1408]{0,1:T(8,128)} %bitcast.203), kind=kLoop, calls=%fused_computation.174 | loop fusion | bytes 1572864 | tf_op jit(solution)/shard_map/stack | solution.py:174
  74.0 0.7 slice.313
  74.7 2.1 %convolution_bitcast_fusion.5 = f32[1,512,256]{2,1,0:T(8,128)} fusion(f32[512,256]{1,0:T(8,128)S(1)} %copy-done.1, f32[256,1408]{0,1:T(8,128)} %bitcast.205), kind=kOutput, calls=%fused_computation.30 | convolution fusion | flops 201326592 | bytes 1310720 | tf_op jit(solution)/shard_map/dot_general | solution.py:40
  76.9 1.1 maximum_maximum_fusion
  78.3 1.1 copy-done.3
  79.4 0.7 multiply_reduce_fusion.3
  80.1 0.4 copy-done.2
  80.4 0.4 convolution_bitcast_fusion.4
  80.9 0.4 convolution_bitcast_fusion.2
  81.3 0.4 convolution_bitcast_fusion.1
  81.7 0.4 convolution_bitcast_fusion.3
  82.1 0.4 convolution_bitcast_fusion
  83.6 0.8 collective-permute-start.1
  84.5 0.8 collective-permute-start.3
  85.3 0.6 dynamic_slice.9
  85.9 0.7 collective-permute-done.2
  86.6 0.7 collective-permute-done.3
  87.5 0.9 copy-done.4
  88.6 0.7 fusion
  89.3 1.4 fusion.105
  90.8 1.4 fusion.103
  92.2 1.5 subtract_add_fusion
  93.8 0.4 subtract_bitcast_fusion.2
  94.1 0.5 add_bitcast_fusion
  94.8 1.4 fusion.106
  96.4 1.5 fusion.104
  97.9 1.6 %subtract_subtract_fusion = f32[768,512]{1,0:T(8,128)S(1)} fusion(f32[768,512]{1,0:T(8,128)S(1)} %fusion.106, f32[768,512]{1,0:T(8,128)S(1)} %get-tuple-element.128, f32[512,512]{1,0:T(8,128)S(1)} %copy-done.6, f32[768,512]{1,0:T(8,128)S(1)} %bitcast.200, f32[768,512]{1,0:T(8,128)S(1)} %bitcast.202), kind=kOutput, calls=%fused_computation.17 | convolution fusion | flops 1209139200 | bytes 8912896 | tf_op jit(solution)/shard_map/dot_general | solution.py:40
  99.5 0.7 multiply_subtract_fusion
  100.6 0.8 pad_maximum_fusion.14
  101.5 0.4 collective-permute-start.6
  102.1 0.7 collective-permute-start.5
  103.0 1.4 collective-permute-done.4
  104.4 0.6 fusion.32
  105.0 1.2 fusion.11
  106.3 0.6 fusion.43
  106.9 1.2 fusion.13
  108.3 0.4 multiply_reduce_fusion.1
  108.9 0.7 pad_maximum_fusion.17
  109.6 0.4 collective-permute-start.7
  110.1 1.1 slice_bitcast_fusion
  111.2 0.6 fusion.54
  111.8 0.6 fusion.14
  112.4 0.7 add_multiply_fusion
  113.3 2.4 %copy.69 = f32[256,1,896]{2,1,0:T(1,128)} copy(f32[256,1,896]{0,2,1:T(8,128)S(1)} %fusion.18) | data formatting | bytes 1835008 | tf_op jit(solution)/shard_map/all_to_all | solution.py:221
  115.7 5.2 %all-to-all-start.1 = ((f32[256,1,896]{2,1,0:T(1,128)}), f32[256,1,896]{2,1,0:T(1,128)S(1)}, u32[]{:S(2)}, u32[]{:S(2)}) async-start(f32[256,1,896]{2,1,0:T(1,128)} %copy.69), calls=%async_computation.1 | async-start | bytes 1835008 | tf_op jit(solution)/shard_map/all_to_all | solution.py:221
  121.2 28.1 %all-to-all-done.1 = f32[256,1,896]{2,1,0:T(1,128)S(1)} async-done(((f32[256,1,896]{2,1,0:T(1,128)}), f32[256,1,896]{2,1,0:T(1,128)S(1)}, u32[]{:S(2)}, u32[]{:S(2)}) %all-to-all-start.1) | async-done | bytes 917536 | tf_op jit(solution)/shard_map/all_to_all | solution.py:221
  149.6 0.4 reshape.279
  150.1 0.5 fusion.94
  151.1 0.5 copy-done.18
  151.6 0.7 bitcast_multiply_fusion.4
  152.5 1.1 fusion.19
  153.6 0.9 copy.77
  154.5 0.7 slice_reduce_fusion
  155.2 0.6 reshape.282
  (123 shorter events, 6.3 us)
Async XLA Ops:
  0.6 6.0 %copy-start.10 = (f32[512,128]{1,0:T(8,128)S(1)}, f32[512,128]{1,0:T(8,128)}, u32[]{:S(2)}) copy-start(f32[512,128]{1,0:T(8,128)} %param.7) | copy-start | bytes 786436
  0.6 6.2 %copy-start.12 = (f32[512,128]{1,0:T(8,128)S(1)}, f32[512,128]{1,0:T(8,128)}, u32[]{:S(2)}) copy-start(f32[512,128]{1,0:T(8,128)} %param.8) | copy-start | bytes 786436
  0.7 6.4 %copy-start.14 = (f32[512,128]{1,0:T(8,128)S(1)}, f32[512,128]{1,0:T(8,128)}, u32[]{:S(2)}) copy-start(f32[512,128]{1,0:T(8,128)} %param.9) | copy-start | bytes 786436
  0.7 6.6 %copy-start.19 = (f32[512,128]{1,0:T(8,128)S(1)}, f32[512,128]{1,0:T(8,128)}, u32[]{:S(2)}) copy-start(f32[512,128]{1,0:T(8,128)} %param.10) | copy-start | bytes 786436
  1.9 5.5 %copy-start.17 = (f32[512,128]{1,0:T(8,128)S(1)}, f32[512,128]{1,0:T(8,128)}, u32[]{:S(2)}) copy-start(f32[512,128]{1,0:T(8,128)} %param.13) | copy-start | bytes 786436
  1.9 5.9 %collective-permute-start = (f32[3,2,128]{2,1,0:T(2,128)S(1)}, f32[3,2,128]{2,1,0:T(2,128)S(1)}, u32[]{:S(2)}, u32[]{:S(2)}) collective-permute-start(f32[3,2,128]{2,1,0:T(2,128)S(1)} %get-tuple-element.97), channel_id=1, source_target_pairs={{0,1},{1,2},{2,3},{3,4},{4,5},{5,6},{6,7},{7,8},{8,9},{9,10},{10,1... | collective-permute-start | bytes 9224 | tf_op jit(solution)/shard_map/ppermute | solution.py:15
  11.4 55.9 %all-to-all-start = ((f32[256,1,1408]{2,1,0:T(1,128)}), f32[256,1,1408]{2,1,0:T(1,128)}, u32[]{:S(2)}, u32[]{:S(2)}) async-start(f32[256,1,1408]{2,1,0:T(1,128)} %all_to_all.22), calls=%async_computation | async-start | bytes 2883584 | tf_op jit(solution)/shard_map/all_to_all | solution.py:171
  37.3 5.9 %copy-start.20 = (f32[3,3,128]{2,1,0:T(4,128)S(1)}, f32[3,3,128]{2,1,0:T(4,128)}, u32[]{:S(2)}) copy-start(f32[3,3,128]{2,1,0:T(4,128)} %param.12) | copy-start | bytes 13828
  72.0 2.7 %copy-start.1 = (f32[512,256]{1,0:T(8,128)S(1)}, f32[512,256]{1,0:T(8,128)}, u32[]{:S(2)}) copy-start(f32[512,256]{1,0:T(8,128)} %get-tuple-element.16) | copy-start | bytes 1572868
  76.9 1.2 copy-start.8
  76.9 1.2 copy-start.9
  78.0 1.4 copy-start.3
  79.4 1.0 copy-start.2
  79.4 1.5 copy-start
  81.7 1.0 copy-start.16
  83.5 1.8 %copy-start.21 = (f32[128]{0:T(128)S(1)}, f32[128]{0:T(128)}, u32[]{:S(2)}) copy-start(f32[128]{0:T(128)} %param.11) | copy-start | bytes 1540
  83.6 2.3 %collective-permute-start.1 = (f32[2,256,256]{2,1,0:T(8,128)S(1)}, f32[2,256,256]{2,1,0:T(8,128)S(1)}, u32[]{:S(2)}, u32[]{:S(2)}) collective-permute-start(f32[2,256,256]{2,1,0:T(8,128)S(1)} %pad_maximum_fusion.9), channel_id=1, source_target_pairs={{0,1},{1,0},{2,3},{3,2},{4,5},{5,4},{6,7},{7,6},{8,9},{9,8},{10,11... | collective-permute-start | bytes 1572872 | tf_op jit(solution)/shard_map/ppermute | solution.py:20
  84.4 2.2 %collective-permute-start.2 = (f32[2,256,256]{2,1,0:T(8,128)S(1)}, f32[2,256,256]{2,1,0:T(8,128)S(1)}, u32[]{:S(2)}, u32[]{:S(2)}) collective-permute-start(f32[2,256,256]{2,1,0:T(8,128)S(1)} %pad_maximum_fusion.10), channel_id=1, source_target_pairs={{0,1},{1,0},{2,3},{3,2},{4,5},{5,4},{6,7},{7,6},{8,9},{9,8},{10,11... | collective-permute-start | bytes 1572872 | tf_op jit(solution)/shard_map/ppermute | solution.py:20
  84.5 2.9 %collective-permute-start.3 = (f32[2,256,256]{2,1,0:T(8,128)S(1)}, f32[2,256,256]{2,1,0:T(8,128)S(1)}, u32[]{:S(2)}, u32[]{:S(2)}) collective-permute-start(f32[2,256,256]{2,1,0:T(8,128)S(1)} %pad_maximum_fusion.11), channel_id=1, source_target_pairs={{0,1},{1,0},{2,3},{3,2},{4,5},{5,4},{6,7},{7,6},{8,9},{9,8},{10,11... | collective-permute-start | bytes 1572872 | tf_op jit(solution)/shard_map/ppermute | solution.py:20
  87.4 1.0 copy-start.4
  87.4 1.2 copy-start.5
  90.8 1.5 copy-start.7
  96.4 1.5 copy-start.6
  101.5 8.7 %collective-permute-start.6 = (f32[2,256,256]{2,1,0:T(8,128)}, f32[2,256,256]{2,1,0:T(8,128)}, u32[]{:S(2)}, u32[]{:S(2)}) collective-permute-start(f32[2,256,256]{2,1,0:T(8,128)} %pad_maximum_fusion.14), channel_id=1, source_target_pairs={{0,1},{1,0},{2,3},{3,2},{4,5},{5,4},{6,7},{7,6},{8,9},{9,8},{10,11... | collective-permute-start | bytes 1572872 | tf_op jit(solution)/shard_map/ppermute | solution.py:20
  101.9 2.5 %collective-permute-start.4 = (f32[2,256,256]{2,1,0:T(8,128)S(1)}, f32[2,256,256]{2,1,0:T(8,128)S(1)}, u32[]{:S(2)}, u32[]{:S(2)}) collective-permute-start(f32[2,256,256]{2,1,0:T(8,128)S(1)} %pad_maximum_fusion.12), channel_id=1, source_target_pairs={{0,1},{1,0},{2,3},{3,2},{4,5},{5,4},{6,7},{7,6},{8,9},{9,8},{10,11... | collective-permute-start | bytes 1572872 | tf_op jit(solution)/shard_map/ppermute | solution.py:20
  102.1 4.2 %collective-permute-start.5 = (f32[2,256,256]{2,1,0:T(8,128)S(1)}, f32[2,256,256]{2,1,0:T(8,128)S(1)}, u32[]{:S(2)}, u32[]{:S(2)}) collective-permute-start(f32[2,256,256]{2,1,0:T(8,128)S(1)} %pad_maximum_fusion.13), channel_id=1, source_target_pairs={{0,1},{1,0},{2,3},{3,2},{4,5},{5,4},{6,7},{7,6},{8,9},{9,8},{10,11... | collective-permute-start | bytes 1572872 | tf_op jit(solution)/shard_map/ppermute | solution.py:20
  109.6 2.8 %collective-permute-start.7 = (f32[10]{0:T(128)S(1)}, f32[10]{0:T(128)S(1)}, u32[]{:S(2)}, u32[]{:S(2)}) collective-permute-start(f32[10]{0:T(128)S(1)} %pad_maximum_fusion.17), channel_id=1, source_target_pairs={{0,1},{1,0},{2,3},{3,2},{4,5},{5,4},{6,7},{7,6},{8,9},{9,8},{10,11... | collective-permute-start | bytes 128 | tf_op jit(solution)/shard_map/ppermute | solution.py:20
  113.3 7.6 %copy-start.11 = (f32[512,128]{1,0:T(8,128)S(1)}, f32[512,128]{1,0:T(8,128)}, u32[]{:S(2)}) copy-start(f32[512,128]{1,0:T(8,128)} %param.7) | copy-start | bytes 786436
  113.3 7.6 %copy-start.13 = (f32[512,128]{1,0:T(8,128)S(1)}, f32[512,128]{1,0:T(8,128)}, u32[]{:S(2)}) copy-start(f32[512,128]{1,0:T(8,128)} %param.8) | copy-start | bytes 786436
  113.3 7.6 %copy-start.15 = (f32[512,128]{1,0:T(8,128)S(1)}, f32[512,128]{1,0:T(8,128)}, u32[]{:S(2)}) copy-start(f32[512,128]{1,0:T(8,128)} %param.9) | copy-start | bytes 786436
  115.7 33.7 %all-to-all-start.1 = ((f32[256,1,896]{2,1,0:T(1,128)}), f32[256,1,896]{2,1,0:T(1,128)S(1)}, u32[]{:S(2)}, u32[]{:S(2)}) async-start(f32[256,1,896]{2,1,0:T(1,128)} %copy.69), calls=%async_computation.1 | async-start | bytes 1835008 | tf_op jit(solution)/shard_map/all_to_all | solution.py:221
  150.6 1.0 copy-start.18

commit v2 on v1

--- a/solution.py
+++ b/solution.py
@@ -86,9 +86,9 @@
 
     keep_real, send_real = split_coarse(first_real)
     keep_imag, send_imag = split_coarse(first_imag)
-    got = [with_partner(jnp.stack([send_real[m], send_imag[m]])) for m in range(members)]
-    full_real = in_halves(first, keep_real, jnp.stack([g[0] for g in got]), 2)
-    full_imag = in_halves(first, keep_imag, jnp.stack([g[1] for g in got]), 2)
+    got_real, got_imag = with_partner(jnp.stack([send_real, send_imag]))
+    full_real = in_halves(first, keep_real, got_real, 2)
+    full_imag = in_halves(first, keep_imag, got_imag, 2)
 
     turned_real = full_real * twiddle_cos + full_imag * twiddle_sin
     turned_imag = full_imag * twiddle_cos - full_real * twiddle_sin

time: 157 us -> 156 us (level)
    ppermute x7 -> x5, waiting for transfers between devices: 2.76 us -> 3.82 us  [with_partner(): return lax.ppermute(block, everyone, [(i, i ^ 1) for i in range(devices)])]
    ppermute x7 -> x5, starting transfers between devices: 3.39 us -> 2.7 us  [with_partner(): return lax.ppermute(block, everyone, [(i, i ^ 1) for i in range(devices)])]
  transfers between devices with their start and end apart: 10 -> 8, of which waited for: 5 -> 4; matrix products, arithmetic and copies ran while one was open for 16% -> 16% of each run, Pallas kernels for 0% -> 0%
where the time goes in v2:
time: 156 us; the launch traced here: 155 us
  waiting for transfers between devices  55.7 us (36%)
  starting transfers between devices  29.9 us (19%)
  other arithmetic  26.4 us (17%)
  local copies, waits for them, and re-layouts  23.3 us (15%)
  matrix products  18 us (12%)
    all_to_all x1, waiting for transfers between devices, on_device(): returned = lax.all_to_all(payload, everyone, 0, 0, tiled=True)  28.1 us
    all_to_all x1, waiting for transfers between devices, on_device(): columns = lax.all_to_all(sent, everyone, 0, 0, tiled=True)  23.8 us
    dot_general x18, matrix products, dot(): return jnp.dot(left, right, precision=exact_mode)  18 us
    all_to_all x1, starting transfers between devices, on_device(): columns = lax.all_to_all(sent, everyone, 0, 0, tiled=True)  17.3 us
    all_to_all x2, local copies, waits for them, and re-layouts, on_device(): columns = lax.all_to_all(sent, everyone, 0, 0, tiled=True)  7.96 us
    add x1, other arithmetic, long_convolutions(): fine_sum = fine_cos + fine_sin  5.86 us
    all_to_all x1, starting transfers between devices, on_device(): returned = lax.all_to_all(payload, everyone, 0, 0, tiled=True)  5.21 us
    ppermute x1, starting transfers between devices, passed_along(): return lax.ppermute(block, axis, route)  4.71 us
  transfers between devices with their start and end apart: 8, of which 4 were waited for; matrix products, arithmetic and copies ran while one was open for 16% of the time, Pallas kernels for 0%

profile of v2, /device:TPU:1, one launch (start us, length us, event | category | flops | bytes accessed | tf_op | source)
XLA Modules:
  0.0 154.9 jit_solution(1433874577381326329)
XLA Ops:
  0.7 1.2 pad_maximum_fusion.5
  1.9 4.7 %collective-permute-start = (f32[3,2,128]{2,1,0:T(2,128)S(1)}, f32[3,2,128]{2,1,0:T(2,128)S(1)}, u32[]{:S(2)}, u32[]{:S(2)}) collective-permute-start(f32[3,2,128]{2,1,0:T(2,128)S(1)} %get-tuple-element.93), channel_id=1, source_target_pairs={{0,1},{1,2},{2,3},{3,4},{4,5},{5,6},{6,7},{7,8},{8,9},{9,10},{10,1... | collective-permute-start | bytes 9224 | tf_op jit(solution)/shard_map/ppermute | solution.py:15
  8.1 3.2 %all_to_all.22 = f32[256,1,1408]{2,1,0:T(1,128)} reshape(f32[128,2,1408]{2,1,0:T(2,128)S(1)} %pad_dynamic-update-slice_fusion) | data formatting | bytes 2883584 | tf_op jit(solution)/shard_map/all_to_all | solution.py:171
  11.4 17.3 %all-to-all-start = ((f32[256,1,1408]{2,1,0:T(1,128)}), f32[256,1,1408]{2,1,0:T(1,128)}, u32[]{:S(2)}, u32[]{:S(2)}) async-start(f32[256,1,1408]{2,1,0:T(1,128)} %all_to_all.22), calls=%async_computation | async-start | bytes 2883584 | tf_op jit(solution)/shard_map/all_to_all | solution.py:171
  28.7 2.1 %fusion.73 = (f32[256,512]{1,0:T(8,128)S(1)}, f32[256,512]{1,0:T(8,128)S(1)}) fusion(s32[512]{0:T(512)S(1)} %iota_add_fusion, s32[256]{0:T(256)S(1)} %iota_add_fusion.2), kind=kLoop, calls=%fused_computation.185 | loop fusion | flops 1835008 | bytes 1051648 | tf_op jit(solution)/shard_map/sin | solution.py:63
  30.8 3.2 %fusion.75 = (f32[512,256]{1,0:T(8,128)}, f32[512,256]{1,0:T(8,128)}) fusion(s32[256]{0:T(256)S(1)} %iota_add_fusion.2, s32[512]{0:T(512)S(1)} %iota_add_fusion), kind=kLoop, calls=%fused_computation.187 | loop fusion | flops 1835008 | bytes 1051648 | tf_op jit(solution)/shard_map/sin | solution.py:60
  34.0 3.2 %fusion.71 = (f32[1,256,512]{2,1,0:T(8,128)}, f32[1,256,512]{2,1,0:T(8,128)}) fusion(s32[512]{0:T(512)S(1)} %iota_add_fusion, s32[256]{0:T(256)S(1)} %iota_add_fusion.1), kind=kLoop, calls=%fused_computation.183 | loop fusion | flops 1835008 | bytes 1051648 | tf_op jit(solution)/shard_map/sin | solution.py:67
  37.2 5.9 %fusion.67 = (f32[512,512]{1,0:T(8,128)}, f32[512,512]{1,0:T(8,128)}, f32[512,512]{1,0:T(8,128)S(1)}, f32[512,512]{1,0:T(8,128)S(1)}) fusion(s32[512]{0:T(512)S(1)} %iota_add_fusion), kind=kLoop, calls=%fused_computation.148 | loop fusion | flops 4194304 | bytes 4196352 | tf_op jit(solution)/shard_map/add | solution.py:72
  43.4 23.8 %all-to-all-done = f32[256,1,1408]{2,1,0:T(1,128)} async-done(((f32[256,1,1408]{2,1,0:T(1,128)}), f32[256,1,1408]{2,1,0:T(1,128)}, u32[]{:S(2)}, u32[]{:S(2)}) %all-to-all-start) | async-done | bytes 1441824 | tf_op jit(solution)/shard_map/all_to_all | solution.py:171
  67.2 4.7 %copy.67 = f32[256,1,1408]{0,2,1:T(8,128)} copy(f32[256,1,1408]{2,1,0:T(1,128)} %all-to-all-done) | data formatting | bytes 2883584 | tf_op jit(solution)/shard_map/all_to_all | solution.py:171
  72.0 2.0 %slice_bitcast_fusion.17 = (f32[1,256,256]{1,2,0:T(8,128)S(1)}, f32[1,256,256]{1,2,0:T(8,128)}, f32[1,256,256]{1,2,0:T(8,128)}) fusion(f32[256,1408]{0,1:T(8,128)} %bitcast.207), kind=kLoop, calls=%fused_computation.170 | loop fusion | bytes 1572864 | tf_op jit(solution)/shard_map/stack | solution.py:174
  74.0 0.7 slice.265
  74.7 2.2 %convolution_bitcast_fusion.5 = f32[1,512,256]{2,1,0:T(8,128)} fusion(f32[512,256]{1,0:T(8,128)S(1)} %copy-done.1, f32[256,1408]{0,1:T(8,128)} %bitcast.209), kind=kOutput, calls=%fused_computation.31 | convolution fusion | flops 201326592 | bytes 1310720 | tf_op jit(solution)/shard_map/dot_general | solution.py:40
  76.9 1.1 maximum_maximum_fusion
  78.0 0.3 multiply_add_fusion.1
  78.3 1.1 copy-done.3
  79.4 0.7 multiply_reduce_fusion.3
  80.1 0.4 copy-done.2
  80.4 0.4 convolution_bitcast_fusion.4
  80.9 0.4 convolution_bitcast_fusion.2
  81.3 0.4 convolution_bitcast_fusion.1
  81.7 0.4 convolution_bitcast_fusion.3
  82.1 0.4 convolution_bitcast_fusion
  83.0 0.2 select_bitcast_fusion
  83.4 1.0 collective-permute-start.1
  84.4 0.6 dynamic_slice.9
  85.0 2.4 %collective-permute-done.1 = f32[2,3,256,256]{3,2,1,0:T(8,128)S(1)} collective-permute-done((f32[2,3,256,256]{3,2,1,0:T(8,128)S(1)}, f32[2,3,256,256]{3,2,1,0:T(8,128)S(1)}, u32[]{:S(2)}, u32[]{:S(2)}) %collective-permute-start.1) | collective-permute-done | bytes 1572896 | tf_op jit(solution)/shard_map/ppermute | solution.py:20
  87.6 0.7 fusion
  88.4 1.4 fusion.101
  89.8 1.4 fusion.99
  91.3 1.5 subtract_add_fusion
  92.8 0.4 subtract_bitcast_fusion.2
  93.2 0.5 add_bitcast_fusion
  93.8 1.4 fusion.102
  95.4 1.5 fusion.100
  96.9 1.6 %subtract_subtract_fusion = f32[768,512]{1,0:T(8,128)S(1)} fusion(f32[768,512]{1,0:T(8,128)S(1)} %fusion.102, f32[768,512]{1,0:T(8,128)S(1)} %get-tuple-element.118, f32[512,512]{1,0:T(8,128)S(1)} %copy-done.6, f32[768,512]{1,0:T(8,128)S(1)} %bitcast.204, f32[768,512]{1,0:T(8,128)S(1)} %bitcast.206), kind=kOutput, calls=%fused_computation.18 | convolution fusion | flops 1209139200 | bytes 8912896 | tf_op jit(solution)/shard_map/dot_general | solution.py:40
  98.5 0.7 multiply_subtract_fusion
  99.7 0.8 pad_maximum_fusion.10
  100.5 0.4 collective-permute-start.4
  100.9 0.2 collective-permute-start.2
  101.2 0.7 collective-permute-start.3
  102.0 1.4 collective-permute-done.2
  103.4 0.6 fusion.32
  104.0 1.2 fusion.11
  105.4 0.6 fusion.43
  106.0 1.2 fusion.13
  107.3 0.4 multiply_reduce_fusion.1
  107.9 0.7 pad_maximum_fusion.13
  108.7 0.4 collective-permute-start.5
  109.2 1.1 slice_bitcast_fusion
  110.2 0.6 fusion.54
  110.8 0.6 fusion.14
  111.5 0.7 add_multiply_fusion
  112.4 2.4 %copy.69 = f32[256,1,896]{2,1,0:T(1,128)} copy(f32[256,1,896]{0,2,1:T(8,128)S(1)} %fusion.18) | data formatting | bytes 1835008 | tf_op jit(solution)/shard_map/all_to_all | solution.py:221
  114.7 5.2 %all-to-all-start.1 = ((f32[256,1,896]{2,1,0:T(1,128)}), f32[256,1,896]{2,1,0:T(1,128)S(1)}, u32[]{:S(2)}, u32[]{:S(2)}) async-start(f32[256,1,896]{2,1,0:T(1,128)} %copy.69), calls=%async_computation.1 | async-start | bytes 1835008 | tf_op jit(solution)/shard_map/all_to_all | solution.py:221
  120.3 28.1 %all-to-all-done.1 = f32[256,1,896]{2,1,0:T(1,128)S(1)} async-done(((f32[256,1,896]{2,1,0:T(1,128)}), f32[256,1,896]{2,1,0:T(1,128)S(1)}, u32[]{:S(2)}, u32[]{:S(2)}) %all-to-all-start.1) | async-done | bytes 917536 | tf_op jit(solution)/shard_map/all_to_all | solution.py:221
  148.7 0.4 reshape.287
  149.1 0.5 fusion.95
  150.1 0.5 copy-done.18
  150.6 0.7 bitcast_multiply_fusion.4
  151.5 1.1 fusion.19
  152.6 0.9 copy.77
  153.5 0.7 slice_reduce_fusion
  154.3 0.6 reshape.290
  (111 shorter events, 5.1 us)
Async XLA Ops:
  0.6 6.0 %copy-start.10 = (f32[512,128]{1,0:T(8,128)S(1)}, f32[512,128]{1,0:T(8,128)}, u32[]{:S(2)}) copy-start(f32[512,128]{1,0:T(8,128)} %param.7) | copy-start | bytes 786436
  0.6 6.2 %copy-start.12 = (f32[512,128]{1,0:T(8,128)S(1)}, f32[512,128]{1,0:T(8,128)}, u32[]{:S(2)}) copy-start(f32[512,128]{1,0:T(8,128)} %param.8) | copy-start | bytes 786436
  0.7 6.4 %copy-start.14 = (f32[512,128]{1,0:T(8,128)S(1)}, f32[512,128]{1,0:T(8,128)}, u32[]{:S(2)}) copy-start(f32[512,128]{1,0:T(8,128)} %param.9) | copy-start | bytes 786436
  0.7 6.6 %copy-start.19 = (f32[512,128]{1,0:T(8,128)S(1)}, f32[512,128]{1,0:T(8,128)}, u32[]{:S(2)}) copy-start(f32[512,128]{1,0:T(8,128)} %param.10) | copy-start | bytes 786436
  1.9 5.5 %copy-start.17 = (f32[512,128]{1,0:T(8,128)S(1)}, f32[512,128]{1,0:T(8,128)}, u32[]{:S(2)}) copy-start(f32[512,128]{1,0:T(8,128)} %param.13) | copy-start | bytes 786436
  1.9 5.9 %collective-permute-start = (f32[3,2,128]{2,1,0:T(2,128)S(1)}, f32[3,2,128]{2,1,0:T(2,128)S(1)}, u32[]{:S(2)}, u32[]{:S(2)}) collective-permute-start(f32[3,2,128]{2,1,0:T(2,128)S(1)} %get-tuple-element.93), channel_id=1, source_target_pairs={{0,1},{1,2},{2,3},{3,4},{4,5},{5,6},{6,7},{7,8},{8,9},{9,10},{10,1... | collective-permute-start | bytes 9224 | tf_op jit(solution)/shard_map/ppermute | solution.py:15
  11.4 55.9 %all-to-all-start = ((f32[256,1,1408]{2,1,0:T(1,128)}), f32[256,1,1408]{2,1,0:T(1,128)}, u32[]{:S(2)}, u32[]{:S(2)}) async-start(f32[256,1,1408]{2,1,0:T(1,128)} %all_to_all.22), calls=%async_computation | async-start | bytes 2883584 | tf_op jit(solution)/shard_map/all_to_all | solution.py:171
  37.2 5.9 %copy-start.20 = (f32[3,3,128]{2,1,0:T(4,128)S(1)}, f32[3,3,128]{2,1,0:T(4,128)}, u32[]{:S(2)}) copy-start(f32[3,3,128]{2,1,0:T(4,128)} %param.12) | copy-start | bytes 13828
  72.0 2.7 %copy-start.1 = (f32[512,256]{1,0:T(8,128)S(1)}, f32[512,256]{1,0:T(8,128)}, u32[]{:S(2)}) copy-start(f32[512,256]{1,0:T(8,128)} %get-tuple-element.16) | copy-start | bytes 1572868
  76.8 1.2 copy-start.8
  76.8 1.2 copy-start.9
  78.0 1.4 copy-start.3
  79.4 1.0 copy-start.2
  79.4 1.5 copy-start
  81.7 1.0 copy-start.16
  83.2 1.2 copy-start.21
  83.4 4.0 %collective-permute-start.1 = (f32[2,3,256,256]{3,2,1,0:T(8,128)S(1)}, f32[2,3,256,256]{3,2,1,0:T(8,128)S(1)}, u32[]{:S(2)}, u32[]{:S(2)}) collective-permute-start(f32[2,3,256,256]{3,2,1,0:T(8,128)S(1)} %pad_maximum_fusion.1), channel_id=1, source_target_pairs={{0,1},{1,0},{2,3},{3,2},{4,5},{5,4},{6,7},{7,6},{8,9},{9,8},{10,11... | collective-permute-start | bytes 4718600 | tf_op jit(solution)/shard_map/ppermute | solution.py:20
  85.0 2.6 %copy-start.4 = (f32[1,256,512]{2,1,0:T(8,128)S(1)}, f32[1,256,512]{2,1,0:T(8,128)}, u32[]{:S(2)}) copy-start(f32[1,256,512]{2,1,0:T(8,128)} %get-tuple-element.19) | copy-start | bytes 1572868
  85.0 2.6 %copy-start.5 = (f32[1,256,512]{2,1,0:T(8,128)S(1)}, f32[1,256,512]{2,1,0:T(8,128)}, u32[]{:S(2)}) copy-start(f32[1,256,512]{2,1,0:T(8,128)} %get-tuple-element.18) | copy-start | bytes 1572868
  89.8 1.5 copy-start.7
  95.4 1.5 copy-start.6
  100.5 8.6 %collective-permute-start.4 = (f32[2,256,256]{2,1,0:T(8,128)}, f32[2,256,256]{2,1,0:T(8,128)}, u32[]{:S(2)}, u32[]{:S(2)}) collective-permute-start(f32[2,256,256]{2,1,0:T(8,128)} %pad_maximum_fusion.10), channel_id=1, source_target_pairs={{0,1},{1,0},{2,3},{3,2},{4,5},{5,4},{6,7},{7,6},{8,9},{9,8},{10,11... | collective-permute-start | bytes 1572872 | tf_op jit(solution)/shard_map/ppermute | solution.py:20
  100.9 2.5 %collective-permute-start.2 = (f32[2,256,256]{2,1,0:T(8,128)S(1)}, f32[2,256,256]{2,1,0:T(8,128)S(1)}, u32[]{:S(2)}, u32[]{:S(2)}) collective-permute-start(f32[2,256,256]{2,1,0:T(8,128)S(1)} %pad_maximum_fusion.8), channel_id=1, source_target_pairs={{0,1},{1,0},{2,3},{3,2},{4,5},{5,4},{6,7},{7,6},{8,9},{9,8},{10,11... | collective-permute-start | bytes 1572872 | tf_op jit(solution)/shard_map/ppermute | solution.py:20
  101.2 4.1 %collective-permute-start.3 = (f32[2,256,256]{2,1,0:T(8,128)S(1)}, f32[2,256,256]{2,1,0:T(8,128)S(1)}, u32[]{:S(2)}, u32[]{:S(2)}) collective-permute-start(f32[2,256,256]{2,1,0:T(8,128)S(1)} %pad_maximum_fusion.9), channel_id=1, source_target_pairs={{0,1},{1,0},{2,3},{3,2},{4,5},{5,4},{6,7},{7,6},{8,9},{9,8},{10,11... | collective-permute-start | bytes 1572872 | tf_op jit(solution)/shard_map/ppermute | solution.py:20
  108.7 2.8 %collective-permute-start.5 = (f32[10]{0:T(128)S(1)}, f32[10]{0:T(128)S(1)}, u32[]{:S(2)}, u32[]{:S(2)}) collective-permute-start(f32[10]{0:T(128)S(1)} %pad_maximum_fusion.13), channel_id=1, source_target_pairs={{0,1},{1,0},{2,3},{3,2},{4,5},{5,4},{6,7},{7,6},{8,9},{9,8},{10,11... | collective-permute-start | bytes 128 | tf_op jit(solution)/shard_map/ppermute | solution.py:20
  112.3 7.7 %copy-start.11 = (f32[512,128]{1,0:T(8,128)S(1)}, f32[512,128]{1,0:T(8,128)}, u32[]{:S(2)}) copy-start(f32[512,128]{1,0:T(8,128)} %param.7) | copy-start | bytes 786436
  112.3 7.7 %copy-start.13 = (f32[512,128]{1,0:T(8,128)S(1)}, f32[512,128]{1,0:T(8,128)}, u32[]{:S(2)}) copy-start(f32[512,128]{1,0:T(8,128)} %param.8) | copy-start | bytes 786436
  112.3 7.7 %copy-start.15 = (f32[512,128]{1,0:T(8,128)S(1)}, f32[512,128]{1,0:T(8,128)}, u32[]{:S(2)}) copy-start(f32[512,128]{1,0:T(8,128)} %param.9) | copy-start | bytes 786436
  114.7 33.7 %all-to-all-start.1 = ((f32[256,1,896]{2,1,0:T(1,128)}), f32[256,1,896]{2,1,0:T(1,128)S(1)}, u32[]{:S(2)}, u32[]{:S(2)}) async-start(f32[256,1,896]{2,1,0:T(1,128)} %copy.69), calls=%async_computation.1 | async-start | bytes 1835008 | tf_op jit(solution)/shard_map/all_to_all | solution.py:221
  149.7 1.0 copy-start.18
